TPU v7x, 256 devices: a whole 4x4x8 slice. The times are simulated.
256 devices in a mesh: dp: 8 (over y, core), expert: 32 (over z, x).
Axes of the slice: x: 4, y: 4, z: 8, core: 2. Of those that a mesh axis runs over, the one named last changes fastest.
Arguments:
- tokens: bfloat16 [4096, 4096], P('expert', 'dp'), may hold values from -6 to 6
- expert_ids: int32 [4096, 8], P('expert'), may hold values from 0 to 63, all different within a row; in each aligned block of 128 rows (0 to 127, 128 to 255, ...) at most 24 rows name the same one
- route_weights: float32 [4096, 8], P('expert'), may hold values from 0.1 to 0.4
- gate_up_weight: bfloat16 [64, 4096, 1536], P('expert', 'dp'), may hold values from -0.09375 to 0.09375
- down_weight: bfloat16 [64, 768, 4096], P('expert', None, 'dp'), may hold values from -0.21875 to 0.21875
- out_grad: bfloat16 [4096, 4096], P('expert', 'dp'), may hold values from -6 to 6
Outputs:
- layer_out: bfloat16 [4096, 4096], P('expert', 'dp')
- token_grad: bfloat16 [4096, 4096], P('expert', 'dp')
- route_grad: float32 [4096, 8], P('expert')
- gate_up_grad: bfloat16 [64, 4096, 1536], P('expert', 'dp')
- down_grad: bfloat16 [64, 768, 4096], P('expert', None, 'dp')
Inputs may be any that keep to these rules, and one draw needn't show every extreme that they name: `expert_ids`: each row names 8 different experts. Among the 128 rows of one group no expert is named more than 24 times, and in every draw some group names some expert exactly 24 times.
All inputs are finite; a program needn't handle non-finite values.
Results may differ from a plain program's by a relative error of at most 0.029.
Values may be sent and summed in bfloat16 or wider, within the bound.
No kernel may reach another device: no remote copies, remote signals or barrier semaphores. Data moves between devices by JAX's collectives and lax.ppermute only.
A program may use at most 128 MiB of HBM per device.

v0:
```python
import jax
import jax.numpy as jnp
from jax import lax
from jax.sharding import PartitionSpec as P


def local(tokens, expert_ids, route_weights, gate_up_weight, down_weight, out_grad):
    tok_count, piece_width = tokens.shape
    top_count = expert_ids.shape[1]
    group_count = lax.axis_size("expert")
    local_count = gate_up_weight.shape[0]
    hidden_units = down_weight.shape[1]
    expert_total = local_count * group_count
    capacity = 3 * tok_count * top_count // (2 * expert_total)
    slot_count = expert_total * capacity
    rows_all = group_count * capacity
    route_count = tok_count * top_count
    block_shape = (local_count, group_count, capacity, piece_width)
    route_ids = expert_ids.reshape(-1)
    onehot = (route_ids[:, None] == jnp.arange(expert_total, dtype=jnp.int32)[None, :]).astype(
        jnp.bfloat16
    )
    order = jnp.arange(route_count, dtype=jnp.int32)
    lower = (order[None, :] < order[:, None]).astype(jnp.bfloat16)
    earlier = jnp.dot(lower, onehot, preferred_element_type=jnp.float32)
    slot_rank = jnp.sum(onehot.astype(jnp.float32) * earlier, axis=1).astype(jnp.int32)
    slot_index = (
        route_ids % local_count * rows_all + route_ids // local_count * capacity + slot_rank
    )
    route_hit = slot_index[:, None] == jnp.arange(slot_count, dtype=jnp.int32)[None, :]
    token_hit = jnp.any(route_hit.reshape(tok_count, top_count, slot_count), axis=1).astype(
        jnp.bfloat16
    )
    weight_flat = route_weights.reshape(-1)
    slot_weight = jnp.sum(jnp.where(route_hit, weight_flat[:, None], 0.0), axis=0)
    outbound = lax.dot_general(
        token_hit, tokens, (((0,), (0,)), ((), ())), preferred_element_type=jnp.float32
    ).astype(jnp.bfloat16)
    grad_outbound = (
        slot_weight[:, None]
        * lax.dot_general(
            token_hit, out_grad, (((0,), (0,)), ((), ())), preferred_element_type=jnp.float32
        )
    ).astype(jnp.bfloat16)
    both = jnp.stack([outbound, grad_outbound]).reshape((2,) + block_shape)
    both = lax.all_to_all(both, "expert", split_axis=2, concat_axis=2, tiled=True)
    arrived = both[0].reshape(local_count, rows_all, piece_width)
    grad_arrived = both[1].reshape(local_count, rows_all, piece_width)
    gate_up_part = jnp.einsum(
        "lrk,lkf->rlf", arrived, gate_up_weight, preferred_element_type=jnp.float32
    ).astype(jnp.bfloat16)
    hidden_grad_part = jnp.einsum(
        "lrk,lfk->rlf", grad_arrived, down_weight, preferred_element_type=jnp.float32
    ).astype(jnp.bfloat16)
    summed = lax.psum_scatter(
        jnp.concatenate([gate_up_part, hidden_grad_part], axis=2),
        "dp",
        scatter_dimension=0,
        tiled=True,
    ).astype(jnp.float32)
    gate_pre = summed[..., :hidden_units]
    up_pre = summed[..., hidden_units : 2 * hidden_units]
    hidden_grad = summed[..., 2 * hidden_units :]
    sigmoid_gate = jax.nn.sigmoid(gate_pre)
    activation = gate_pre * sigmoid_gate
    hidden_mine = (activation * up_pre).astype(jnp.bfloat16)
    gate_grad = hidden_grad * up_pre * sigmoid_gate * (1.0 + gate_pre * (1.0 - sigmoid_gate))
    up_grad = hidden_grad * activation
    preact_grad = jnp.concatenate([gate_grad, up_grad], axis=2).astype(jnp.bfloat16)
    hidden_all = lax.all_gather(hidden_mine, "dp", axis=0, tiled=True)
    preact_grad_all = lax.all_gather(preact_grad, "dp", axis=0, tiled=True)
    out_slice = jnp.einsum(
        "rlf,lfk->lrk", hidden_all, down_weight, preferred_element_type=jnp.float32
    ).astype(jnp.bfloat16)
    grad_routes = jnp.repeat(out_grad, top_count, axis=0).astype(jnp.float32)
    returned = lax.all_to_all(
        out_slice.reshape(block_shape), "expert", split_axis=1, concat_axis=1, tiled=True
    )
    route_pick = route_hit.astype(jnp.bfloat16)
    y_routes = jnp.dot(
        route_pick, returned.reshape(slot_count, piece_width), preferred_element_type=jnp.float32
    )
    layer_out = (
        (weight_flat[:, None] * y_routes)
        .reshape(tok_count, top_count, piece_width)
        .sum(axis=1)
        .astype(jnp.bfloat16)
    )
    partial_dot = jnp.sum(grad_routes * y_routes, axis=1).reshape(tok_count, top_count)
    route_grad = lax.psum(partial_dot, "dp")
    x_grad_slice = jnp.einsum(
        "rlf,lkf->lrk", preact_grad_all, gate_up_weight, preferred_element_type=jnp.float32
    ).astype(jnp.bfloat16)
    gate_up_grad = jnp.einsum(
        "lrk,rlf->lkf", arrived, preact_grad_all, preferred_element_type=jnp.float32
    ).astype(jnp.bfloat16)
    down_grad = jnp.einsum(
        "rlf,lrk->lfk", hidden_all, grad_arrived, preferred_element_type=jnp.float32
    ).astype(jnp.bfloat16)
    grad_back = lax.all_to_all(
        x_grad_slice.reshape(block_shape), "expert", split_axis=1, concat_axis=1, tiled=True
    )
    token_grad = jnp.dot(
        token_hit, grad_back.reshape(slot_count, piece_width), preferred_element_type=jnp.float32
    ).astype(jnp.bfloat16)
    return (layer_out, token_grad, route_grad, gate_up_grad, down_grad)


def solution(mesh):
    placed = (
        P("expert", "dp"),
        P("expert", None),
        P("expert", None),
        P("expert", "dp", None),
        P("expert", None, "dp"),
        P("expert", "dp"),
    )
    return jax.shard_map(
        local,
        mesh=mesh,
        in_specs=placed,
        out_specs=(
            P("expert", "dp"),
            P("expert", "dp"),
            P("expert", None),
            P("expert", "dp", None),
            P("expert", None, "dp"),
        ),
        check_vma=False,
    )
```

profile of v0, /device:TPU:4, one launch (start us, length us, event | category | flops | bytes accessed | tf_op | source)
XLA Modules:
  0.0 303.9 jit_solution(3204589052721626172)
XLA Ops:
  7.2 0.9 copy.56
  8.3 0.6 fusion.7
  8.9 0.8 copy.55
  9.9 3.2 %fusion.1 = pred[128,1536]{1,0:T(8,128)(4,1)S(1)} fusion(s32[128,8]{1,0:T(8,128)S(1)} %fusion.13), kind=kLoop, calls=%fused_computation.5 | loop fusion | flops 2949120 | bytes 200704 | tf_op jit(solution)/shard_map/reduce_or | solution.py:31
  13.1 0.8 select_reduce_fusion
  13.9 1.5 convolution_convert_fusion.1
  15.5 0.6 fusion.4
  16.9 84.4 %all_to_all.15 = bf16[2,2,32,24,512]{4,3,1,0,2:T(8,128)(2,1)S(1)} all-to-all(bf16[2,2,32,24,512]{4,3,1,0,2:T(8,128)(2,1)S(1)} %copy.74), channel_id=1, replica_groups=mesh['dp'=8,'expert'=32] {'expert'}, dimensions={2} | all-to-all | bytes 6291456 | tf_op jit(solution)/shard_map/all_to_all | solution.py:46
  101.8 4.2 %convert_bitcast_fusion = bf16[768,2,1536]{2,0,1:T(8,128)(2,1)} fusion(bf16[2,768,512]{2,1,0:T(8,128)(2,1)S(1)} %bitcast.40, bf16[2,512,1536]{2,1,0:T(8,128)(2,1)S(1)} %copy-done), kind=kOutput, calls=%fused_computation.6 | convolution fusion | flops 2418278400 | bytes 9437184 | tf_op jit(solution)/shard_map/lrk,lkf->rlf/dot_general | solution.py:49
  106.0 2.8 convert_bitcast_fusion.1
  108.9 6.4 %pad_maximum_fusion = bf16[768,2,2304]{2,0,1:T(8,128)(2,1)} fusion(bf16[768,2,768]{2,0,1:T(8,128)(2,1)} %convert_bitcast_fusion.1, bf16[768,2,1536]{2,0,1:T(8,128)(2,1)} %convert_bitcast_fusion), kind=kLoop, calls=%fused_computation | loop fusion | flops 14155776 | bytes 14155776 | tf_op jit(solution)/shard_map/concatenate | solution.py:56
  115.4 45.8 %reduce-scatter.2.cloned.1.call-done = bf16[96,2,2304]{2,0,1:T(8,128)(2,1)} async-done(((bf16[768,2,2304]{2,0,1:T(8,128)(2,1)}), bf16[96,2,2304]{2,0,1:T(8,128)(2,1)}) %reduce-scatter.2.cloned.1.call-update) | async-done | bytes 884752 | tf_op jit(solution)/shard_map/reduce_scatter | solution.py:55
  161.2 1.3 convert_element_type.80
  162.5 1.2 multiply_convert_fusion.1
  163.7 1.9 pad_maximum_fusion.2
  165.6 26.0 %all-gather.3.cloned.1.call-done = bf16[768,2,768]{2,0,1:T(8,128)(2,1)} async-done(((bf16[96,2,768]{2,0,1:T(8,128)(2,1)}), bf16[768,2,768]{2,0,1:T(8,128)(2,1)}) %all-gather.3.cloned.1.call-update) | async-done | bytes 2359312 | tf_op jit(solution)/shard_map/all_gather | solution.py:70
  191.6 3.5 %convolution_convert_fusion.3 = bf16[2,768,512]{2,1,0:T(8,128)(2,1)S(1)} fusion(bf16[768,2,768]{2,0,1:T(8,128)(2,1)} %all-gather.3.cloned.1.call-done, bf16[2,768,512]{2,1,0:T(8,128)(2,1)} %param.10), kind=kOutput, calls=%fused_computation.20 | convolution fusion | flops 1208745984 | bytes 5505024 | tf_op jit(solution)/shard_map/rlf,lfk->lrk/dot_general | solution.py:72
  195.1 1.4 copy.66
  196.5 10.2 %all-to-all-start.1 = ((bf16[2,32,24,512]{3,2,0,1:T(8,128)(2,1)}), bf16[2,32,24,512]{3,2,0,1:T(8,128)(2,1)}, u32[]{:S(2)}, u32[]{:S(2)}) async-start(bf16[2,32,24,512]{3,2,0,1:T(8,128)(2,1)} %copy.66), calls=%async_computation.2 | async-start | bytes 3145728 | tf_op jit(solution)/shard_map/all_to_all | solution.py:76
  206.7 24.8 %all-gather.5.cloned.1.call-done = bf16[768,2,1536]{2,0,1:T(8,128)(2,1)} async-done(((bf16[96,2,1536]{2,0,1:T(8,128)(2,1)}), bf16[768,2,1536]{2,0,1:T(8,128)(2,1)}) %all-gather.5.cloned.1.call-update) | async-done | bytes 4718608 | tf_op jit(solution)/shard_map/all_gather | solution.py:71
  231.4 5.0 %convolution_convert_fusion.4 = bf16[2,768,512]{2,1,0:T(8,128)(2,1)S(1)} fusion(bf16[768,2,1536]{2,0,1:T(8,128)(2,1)} %all-gather.5.cloned.1.call-done, bf16[2,512,1536]{2,1,0:T(8,128)(2,1)S(1)} %copy-done), kind=kOutput, calls=%fused_computation.21 | convolution fusion | flops 2416705536 | bytes 9437184 | tf_op jit(solution)/shard_map/rlf,lkf->lrk/dot_general | solution.py:91
  236.4 1.4 copy.68
  237.8 8.6 %all-to-all-done.1 = bf16[2,32,24,512]{3,2,0,1:T(8,128)(2,1)} async-done(((bf16[2,32,24,512]{3,2,0,1:T(8,128)(2,1)}), bf16[2,32,24,512]{3,2,0,1:T(8,128)(2,1)}, u32[]{:S(2)}, u32[]{:S(2)}) %all-to-all-start.1) | async-done | bytes 1572896 | tf_op jit(solution)/shard_map/all_to_all | solution.py:76
  246.4 5.6 %all-to-all-start.2 = ((bf16[2,32,24,512]{3,2,0,1:T(8,128)(2,1)}), bf16[2,32,24,512]{3,2,0,1:T(8,128)(2,1)}, u32[]{:S(2)}, u32[]{:S(2)}) async-start(bf16[2,32,24,512]{3,2,0,1:T(8,128)(2,1)} %copy.68), calls=%async_computation.3 | async-start | bytes 3145728 | tf_op jit(solution)/shard_map/all_to_all | solution.py:100
  252.0 4.7 %convolution_convert_fusion.2 = bf16[2,768,512]{2,1,0:T(8,128)(2,1)} fusion(bf16[768,2,768]{2,0,1:T(8,128)(2,1)} %all-gather.3.cloned.1.call-done, bf16[2,768,512]{2,1,0:T(8,128)(2,1)} %bitcast.43), kind=kOutput, calls=%fused_computation.19 | convolution fusion | flops 1208745984 | bytes 5505024 | tf_op jit(solution)/shard_map/rlf,lrk->lfk/dot_general | solution.py:97
  256.7 1.5 copy.67
  258.3 2.9 bitcast_reduce_fusion
  261.5 25.5 %psum.7 = f32[128,8]{1,0:T(8,128)S(1)} all-reduce(f32[128,8]{1,0:T(8,128)S(1)} %reshape.113), channel_id=1, replica_groups=mesh['dp'=8,'expert'=32] {'dp'}, use_global_device_ids=true, to_apply=%region_6.7 | all-reduce | flops 1024 | bytes 8192 | tf_op jit(solution)/shard_map/psum | solution.py:90
  287.1 0.7 copy.71
  287.7 7.1 %convolution_convert_fusion = bf16[2,512,1536]{2,1,0:T(8,128)(2,1)} fusion(bf16[2,768,512]{2,1,0:T(8,128)(2,1)} %bitcast.41, bf16[768,2,1536]{2,0,1:T(8,128)(2,1)} %all-gather.5.cloned.1.call-done), kind=kOutput, calls=%fused_computation.9 | convolution fusion | flops 2417491968 | bytes 9437184 | tf_op jit(solution)/shard_map/lrk,rlf->lkf/dot_general | solution.py:94
  294.8 1.5 copy.69
  296.4 1.0 convolution_convert_fusion.5
  (31 shorter events, 2.2 us)
Async XLA Ops:
  7.2 94.6 %copy-start = (bf16[2,512,1536]{2,1,0:T(8,128)(2,1)S(1)}, bf16[2,512,1536]{2,1,0:T(8,128)(2,1)}, u32[]{:S(2)}) copy-start(bf16[2,512,1536]{2,1,0:T(8,128)(2,1)} %param.9) | copy-start | bytes 9437188
  7.2 154.0 %reduce-scatter.2.cloned.1.call-start = ((), (), s32[]{:S(2)}) async-start(), calls=%async_computation.4 | async-start | bytes 7962624 | tf_op jit(solution)/shard_map/reduce_scatter | solution.py:55
  8.3 7.2 %copy-start.3 = (bf16[128,512]{1,0:T(8,128)(2,1)S(1)}, bf16[128,512]{1,0:T(8,128)(2,1)}, u32[]{:S(2)}) copy-start(bf16[128,512]{1,0:T(8,128)(2,1)} %param.11) | copy-start | bytes 393220
  101.7 4.4 %copy-start.1 = (bf16[1,2,32,24,512]{4,3,2,1,0:T(8,128)(2,1)}, bf16[1,2,32,24,512]{4,3,2,1,0:T(8,128)(2,1)S(1)}, u32[]{:S(2)}) copy-start(bf16[1,2,32,24,512]{4,3,2,1,0:T(8,128)(2,1)S(1)} %copy.63) | copy-start | bytes 4718596
  101.8 4.2 %copy-start.2 = (bf16[1,2,32,24,512]{4,3,2,1,0:T(8,128)(2,1)}, bf16[1,2,32,24,512]{4,3,2,1,0:T(8,128)(2,1)S(1)}, u32[]{:S(2)}) copy-start(bf16[1,2,32,24,512]{4,3,2,1,0:T(8,128)(2,1)S(1)} %copy.64) | copy-start | bytes 4718596
  101.8 4.2 %copy-start.4 = (bf16[2,768,512]{2,1,0:T(8,128)(2,1)S(1)}, bf16[2,768,512]{2,1,0:T(8,128)(2,1)}, u32[]{:S(2)}) copy-start(bf16[2,768,512]{2,1,0:T(8,128)(2,1)} %param.10) | copy-start | bytes 4718596
  115.3 76.3 %all-gather.3.cloned.1.call-start = ((), (), s32[]{:S(2)}) async-start(), calls=%async_computation.5 | async-start | bytes 2654208 | tf_op jit(solution)/shard_map/all_gather | solution.py:70
  163.7 67.8 %all-gather.5.cloned.1.call-start = ((), (), s32[]{:S(2)}) async-start(), calls=%async_computation.6 | async-start | bytes 5308416 | tf_op jit(solution)/shard_map/all_gather | solution.py:71
  196.5 49.9 %all-to-all-start.1 = ((bf16[2,32,24,512]{3,2,0,1:T(8,128)(2,1)}), bf16[2,32,24,512]{3,2,0,1:T(8,128)(2,1)}, u32[]{:S(2)}, u32[]{:S(2)}) async-start(bf16[2,32,24,512]{3,2,0,1:T(8,128)(2,1)} %copy.66), calls=%async_computation.2 | async-start | bytes 3145728 | tf_op jit(solution)/shard_map/all_to_all | solution.py:76
  246.4 48.4 %all-to-all-start.2 = ((bf16[2,32,24,512]{3,2,0,1:T(8,128)(2,1)}), bf16[2,32,24,512]{3,2,0,1:T(8,128)(2,1)}, u32[]{:S(2)}, u32[]{:S(2)}) async-start(bf16[2,32,24,512]{3,2,0,1:T(8,128)(2,1)} %copy.68), calls=%async_computation.3 | async-start | bytes 3145728 | tf_op jit(solution)/shard_map/all_to_all | solution.py:100
Sparse Core Ops, SparseCore 0:
  115.4 45.7 reduce-scatter.1
  163.8 27.7 all-gather.2
  194.0 37.3 all-gather.4
where the time goes:
time: 304 us
  blocking collectives  110 us (36%)
  waiting for transfers between devices  105 us (35%)
  matrix products  34 us (11%)
  starting transfers between devices  15.9 us (5%)
  other arithmetic  15.4 us (5%)
  between operations  14 us (5%)
  local copies, waits for them, and re-layouts  9.53 us (3%)
    all_to_all x1, blocking collectives, local(): lax.all_to_all(both, 'expert', split_axis=2, concat_axis=2, tiled=True)  84.4 us
    reduce_scatter x1, waiting for transfers between devices, local(): lax.psum_scatter(jnp.concatenate([gate_up_part, hidden_grad_part], axis=2...  45.8 us
    all_gather x1, waiting for transfers between devices, local(): hidden_all = lax.all_gather(hidden_mine, 'dp', axis=0, tiled=True)  26 us
    psum x1, blocking collectives, local(): route_grad = lax.psum(partial_dot, 'dp')  25.5 us
    all_gather x1, waiting for transfers between devices, local(): preact_grad_all = lax.all_gather(preact_grad, 'dp', axis=0, tiled=True)  24.8 us
    all_to_all x1, starting transfers between devices, local(): lax.all_to_all(out_slice.reshape(block_shape), 'expert', split_axis=1, co...  10.2 us
    all_to_all x1, waiting for transfers between devices, local(): lax.all_to_all(out_slice.reshape(block_shape), 'expert', split_axis=1, co...  8.58 us
    dot_general x1, matrix products, local(): jnp.einsum('lrk,rlf->lkf', arrived, preact_grad_all, preferred_element_ty...  7.12 us
  transfers between devices with their start and end apart: 5, of which 4 were waited for; matrix products, arithmetic and copies ran while one was open for 10% of the time, Pallas kernels for 0%

commit v1 on v0

--- a/solution.py
+++ b/solution.py
@@ -67,7 +67,9 @@
     gate_grad = hidden_grad * up_pre * sigmoid_gate * (1.0 + gate_pre * (1.0 - sigmoid_gate))
     up_grad = hidden_grad * activation
     preact_grad = jnp.concatenate([gate_grad, up_grad], axis=2).astype(jnp.bfloat16)
-    hidden_all = lax.all_gather(hidden_mine, "dp", axis=0, tiled=True)
+    hidden_all = jnp.concatenate(
+        jax.lax.all_to_all(jnp.stack(jax.lax.axis_size("dp") * [hidden_mine]), "dp", 0, 0), axis=0
+    )
     preact_grad_all = lax.all_gather(preact_grad, "dp", axis=0, tiled=True)
     out_slice = jnp.einsum(
         "rlf,lfk->lrk", hidden_all, down_weight, preferred_element_type=jnp.float32

time: 304 us -> 328 us (1.079)
  blocking collectives: 110 us -> 160 us
  waiting for transfers between devices: 105 us -> 77.3 us
    all_to_all x0 -> x1, blocking collectives: none -> 50.4 us  [local(): jax.lax.all_to_all(jnp.stack(jax.lax.axis_size('dp') * [hidden_mine]), 'd...]
    all_gather x1 -> x0, waiting for transfers between devices: 26 us -> none  [local(): hidden_all = lax.all_gather(hidden_mine, 'dp', axis=0, tiled=True)]
    all_gather x1, waiting for transfers between devices: 24.8 us -> 0.02 us  [local(): preact_grad_all = lax.all_gather(preact_grad, 'dp', axis=0, tiled=True)]
    all_to_all x1, waiting for transfers between devices: 8.58 us -> 31.5 us  [local(): lax.all_to_all(out_slice.reshape(block_shape), 'expert', split_axis=1, co...]
  transfers between devices with their start and end apart: 5 -> 4, of which waited for: 4 -> 2; matrix products, arithmetic and copies ran while one was open for 10% -> 8% of each run, Pallas kernels for 0% -> 0%
where the time goes in v1:
time: 328 us; the launch traced here: 327 us
  blocking collectives  160 us (49%)
  waiting for transfers between devices  77.3 us (24%)
  matrix products  31.9 us (10%)
  starting transfers between devices  16.4 us (5%)
  between operations  14.3 us (4%)
  other arithmetic  14.2 us (4%)
  local copies, waits for them, and re-layouts  12.8 us (4%)
    all_to_all x1, blocking collectives, local(): lax.all_to_all(both, 'expert', split_axis=2, concat_axis=2, tiled=True)  84.4 us
    all_to_all x1, blocking collectives, local(): jax.lax.all_to_all(jnp.stack(jax.lax.axis_size('dp') * [hidden_mine]), 'd...  50.4 us
    reduce_scatter x1, waiting for transfers between devices, local(): lax.psum_scatter(jnp.concatenate([gate_up_part, hidden_grad_part], axis=2...  45.8 us
    all_to_all x1, waiting for transfers between devices, local(): lax.all_to_all(out_slice.reshape(block_shape), 'expert', split_axis=1, co...  31.5 us
    psum x1, blocking collectives, local(): route_grad = lax.psum(partial_dot, 'dp')  25.5 us
    all_to_all x1, starting transfers between devices, local(): lax.all_to_all(out_slice.reshape(block_shape), 'expert', split_axis=1, co...  10.2 us
    dot_general x1, matrix products, local(): jnp.einsum('lrk,rlf->lkf', arrived, preact_grad_all, preferred_element_ty...  7.12 us
  transfers between devices with their start and end apart: 4, of which 2 were waited for; matrix products, arithmetic and copies ran while one was open for 8% of the time, Pallas kernels for 0%

profile of v1, /device:TPU:4, one launch (start us, length us, event | category | flops | bytes accessed | tf_op | source)
XLA Modules:
  0.0 327.2 jit_solution(7728983033630526296)
XLA Ops:
  7.2 0.9 copy.62
  8.9 0.8 copy.61
  10.0 3.2 fusion.1
  13.1 0.8 select_reduce_fusion
  13.9 1.5 convolution_convert_fusion.1
  15.5 0.6 fusion.4
  16.9 84.4 %all_to_all.20 = bf16[2,2,32,24,512]{4,3,1,0,2:T(8,128)(2,1)S(1)} all-to-all(bf16[2,2,32,24,512]{4,3,1,0,2:T(8,128)(2,1)S(1)} %copy.83), channel_id=1, replica_groups=mesh['dp'=8,'expert'=32] {'expert'}, dimensions={2} | all-to-all | bytes 6291456 | tf_op jit(solution)/shard_map/all_to_all | solution.py:46
  101.8 4.2 %convert_bitcast_fusion = bf16[768,2,1536]{2,0,1:T(8,128)(2,1)} fusion(bf16[2,768,512]{2,1,0:T(8,128)(2,1)S(1)} %bitcast.43, bf16[2,512,1536]{2,1,0:T(8,128)(2,1)S(1)} %copy-done), kind=kOutput, calls=%fused_computation.6 | convolution fusion | flops 2418278400 | bytes 9437184 | tf_op jit(solution)/shard_map/lrk,lkf->rlf/dot_general | solution.py:49
  106.1 2.8 convert_bitcast_fusion.1
  108.9 6.4 %pad_maximum_fusion = bf16[768,2,2304]{2,0,1:T(8,128)(2,1)} fusion(bf16[768,2,768]{2,0,1:T(8,128)(2,1)} %convert_bitcast_fusion.1, bf16[768,2,1536]{2,0,1:T(8,128)(2,1)} %convert_bitcast_fusion), kind=kLoop, calls=%fused_computation | loop fusion | flops 14155776 | bytes 14155776 | tf_op jit(solution)/shard_map/concatenate | solution.py:56
  115.4 45.8 %reduce-scatter.2.cloned.1.call-done = bf16[96,2,2304]{2,0,1:T(8,128)(2,1)} async-done(((bf16[768,2,2304]{2,0,1:T(8,128)(2,1)}), bf16[96,2,2304]{2,0,1:T(8,128)(2,1)}) %reduce-scatter.2.cloned.1.call-update) | async-done | bytes 884752 | tf_op jit(solution)/shard_map/reduce_scatter | solution.py:55
  161.2 1.3 convert_element_type.80
  162.5 1.0 multiply_convert_fusion.1
  163.5 0.8 pad_maximum_fusion.2
  164.4 1.2 stack.11
  165.6 50.4 %all_to_all.21 = bf16[8,96,2,768]{3,1,2,0:T(8,128)(2,1)S(1)} all-to-all(bf16[8,96,2,768]{3,1,2,0:T(8,128)(2,1)S(1)} %stack.11), channel_id=1, replica_groups=mesh['dp'=8,'expert'=32] {'dp'}, dimensions={0} | all-to-all | bytes 4718592 | tf_op jit(solution)/shard_map/all_to_all | solution.py:71
  216.2 1.9 copy-done.6
  218.1 1.4 convolution_convert_fusion.3
  219.5 1.4 copy.73
  220.9 10.2 %all-to-all-start.2 = ((bf16[2,32,24,512]{3,2,0,1:T(8,128)(2,1)}), bf16[2,32,24,512]{3,2,0,1:T(8,128)(2,1)}, u32[]{:S(2)}, u32[]{:S(2)}) async-start(bf16[2,32,24,512]{3,2,0,1:T(8,128)(2,1)} %copy.73), calls=%async_computation.3 | async-start | bytes 3145728 | tf_op jit(solution)/shard_map/all_to_all | solution.py:78
  231.1 5.0 %convolution_convert_fusion.4 = bf16[2,768,512]{2,1,0:T(8,128)(2,1)S(1)} fusion(bf16[768,2,1536]{2,0,1:T(8,128)(2,1)} %all-gather.2.cloned.1.call-done, bf16[2,512,1536]{2,1,0:T(8,128)(2,1)S(1)} %copy-done), kind=kOutput, calls=%fused_computation.21 | convolution fusion | flops 2416705536 | bytes 9437184 | tf_op jit(solution)/shard_map/rlf,lkf->lrk/dot_general | solution.py:93
  236.1 1.4 copy.75
  237.4 31.5 %all-to-all-done.2 = bf16[2,32,24,512]{3,2,0,1:T(8,128)(2,1)} async-done(((bf16[2,32,24,512]{3,2,0,1:T(8,128)(2,1)}), bf16[2,32,24,512]{3,2,0,1:T(8,128)(2,1)}, u32[]{:S(2)}, u32[]{:S(2)}) %all-to-all-start.2) | async-done | bytes 1572896 | tf_op jit(solution)/shard_map/all_to_all | solution.py:78
  268.9 6.1 %all-to-all-start.3 = ((bf16[2,32,24,512]{3,2,0,1:T(8,128)(2,1)}), bf16[2,32,24,512]{3,2,0,1:T(8,128)(2,1)}, u32[]{:S(2)}, u32[]{:S(2)}) async-start(bf16[2,32,24,512]{3,2,0,1:T(8,128)(2,1)} %copy.75), calls=%async_computation.4 | async-start | bytes 3145728 | tf_op jit(solution)/shard_map/all_to_all | solution.py:102
  275.0 4.7 %convolution_convert_fusion.2 = bf16[2,768,512]{2,1,0:T(8,128)(2,1)} fusion(bf16[768,2,768]{2,0,1:T(8,128)(2,1)} %bitcast.42, bf16[2,768,512]{2,1,0:T(8,128)(2,1)} %bitcast.46), kind=kOutput, calls=%fused_computation.19 | convolution fusion | flops 1208745984 | bytes 5505024 | tf_op jit(solution)/shard_map/rlf,lrk->lfk/dot_general | solution.py:99
  279.7 1.5 copy.74
  281.3 2.9 bitcast_reduce_fusion
  284.5 25.5 %psum.7 = f32[128,8]{1,0:T(8,128)S(1)} all-reduce(f32[128,8]{1,0:T(8,128)S(1)} %reshape.119), channel_id=1, replica_groups=mesh['dp'=8,'expert'=32] {'dp'}, use_global_device_ids=true, to_apply=%region_6.7 | all-reduce | flops 1024 | bytes 8192 | tf_op jit(solution)/shard_map/psum | solution.py:92
  310.1 0.7 copy.79
  310.7 7.1 %convolution_convert_fusion = bf16[2,512,1536]{2,1,0:T(8,128)(2,1)} fusion(bf16[2,768,512]{2,1,0:T(8,128)(2,1)} %bitcast.44, bf16[768,2,1536]{2,0,1:T(8,128)(2,1)} %all-gather.2.cloned.1.call-done), kind=kOutput, calls=%fused_computation.9 | convolution fusion | flops 2417491968 | bytes 9437184 | tf_op jit(solution)/shard_map/lrk,rlf->lkf/dot_general | solution.py:96
  317.8 1.5 copy.76
  319.4 1.0 convolution_convert_fusion.5
  (35 shorter events, 2.9 us)
Async XLA Ops:
  7.2 94.7 %copy-start = (bf16[2,512,1536]{2,1,0:T(8,128)(2,1)S(1)}, bf16[2,512,1536]{2,1,0:T(8,128)(2,1)}, u32[]{:S(2)}) copy-start(bf16[2,512,1536]{2,1,0:T(8,128)(2,1)} %param.9) | copy-start | bytes 9437188
  7.2 8.3 %copy-start.4 = (bf16[128,512]{1,0:T(8,128)(2,1)S(1)}, bf16[128,512]{1,0:T(8,128)(2,1)}, u32[]{:S(2)}) copy-start(bf16[128,512]{1,0:T(8,128)(2,1)} %param.11) | copy-start | bytes 393220
  7.2 154.0 %reduce-scatter.2.cloned.1.call-start = ((), (), s32[]{:S(2)}) async-start(), calls=%async_computation.5 | async-start | bytes 7962624 | tf_op jit(solution)/shard_map/reduce_scatter | solution.py:55
  101.7 4.4 %copy-start.2 = (bf16[1,2,32,24,512]{4,3,2,1,0:T(8,128)(2,1)}, bf16[1,2,32,24,512]{4,3,2,1,0:T(8,128)(2,1)S(1)}, u32[]{:S(2)}) copy-start(bf16[1,2,32,24,512]{4,3,2,1,0:T(8,128)(2,1)S(1)} %copy.69) | copy-start | bytes 4718596
  101.8 4.2 %copy-start.3 = (bf16[1,2,32,24,512]{4,3,2,1,0:T(8,128)(2,1)}, bf16[1,2,32,24,512]{4,3,2,1,0:T(8,128)(2,1)S(1)}, u32[]{:S(2)}) copy-start(bf16[1,2,32,24,512]{4,3,2,1,0:T(8,128)(2,1)S(1)} %copy.70) | copy-start | bytes 4718596
  101.8 4.2 %copy-start.5 = (bf16[2,768,512]{2,1,0:T(8,128)(2,1)S(1)}, bf16[2,768,512]{2,1,0:T(8,128)(2,1)}, u32[]{:S(2)}) copy-start(bf16[2,768,512]{2,1,0:T(8,128)(2,1)} %param.10) | copy-start | bytes 4718596
  115.3 115.7 %all-gather.2.cloned.1.call-start = ((), (), s32[]{:S(2)}) async-start(), calls=%async_computation.6 | async-start | bytes 5308416 | tf_op jit(solution)/shard_map/all_gather | solution.py:73
  216.0 2.1 copy-start.6
  216.2 3.3 %copy-start.1 = (bf16[8,96,2,768]{3,1,0,2:T(8,128)(2,1)}, bf16[8,96,2,768]{3,1,0,2:T(8,128)(2,1)S(1)}, u32[]{:S(2)}) copy-start(bf16[8,96,2,768]{3,1,0,2:T(8,128)(2,1)S(1)} %copy.72) | copy-start | bytes 7077892
  220.9 48.0 %all-to-all-start.2 = ((bf16[2,32,24,512]{3,2,0,1:T(8,128)(2,1)}), bf16[2,32,24,512]{3,2,0,1:T(8,128)(2,1)}, u32[]{:S(2)}, u32[]{:S(2)}) async-start(bf16[2,32,24,512]{3,2,0,1:T(8,128)(2,1)} %copy.73), calls=%async_computation.3 | async-start | bytes 3145728 | tf_op jit(solution)/shard_map/all_to_all | solution.py:78
  268.9 49.0 %all-to-all-start.3 = ((bf16[2,32,24,512]{3,2,0,1:T(8,128)(2,1)}), bf16[2,32,24,512]{3,2,0,1:T(8,128)(2,1)}, u32[]{:S(2)}, u32[]{:S(2)}) async-start(bf16[2,32,24,512]{3,2,0,1:T(8,128)(2,1)} %copy.75), calls=%async_computation.4 | async-start | bytes 3145728 | tf_op jit(solution)/shard_map/all_to_all | solution.py:102
Sparse Core Ops, SparseCore 0:
  115.5 45.7 reduce-scatter.1
  164.5 53.7 all-gather.1
